TPU v7x, 512 devices: a whole 4x8x8 slice. The times are simulated.
512 devices in a mesh: page: 32 (over y_lo, z), req: 16 (over y_hi, x, core).
Axes of the slice: x: 4, y: 8 (y_hi: 2, y_lo: 4; y = y_hi * 4 + y_lo), z: 8, core: 2. Of those that a mesh axis runs over, the one named last changes fastest.
Arguments:
- queries: bfloat16 [256, 8192], P('req'), may hold values from -250 to 250
- key_pool: bfloat16 [512, 128, 1024], P(('page', 'req')), may hold values from -6 to 6
- value_pool: bfloat16 [512, 128, 1024], P(('page', 'req')), may hold values from -6 to 6
- page_table: int32 [256, 32], P('req'), may hold values from 0 to 511, as said below
- page_count: int32 [256], P('req'), may hold values from 1 to 32, as said below
Outputs:
- attended: bfloat16 [256, 8192], P('req', 'page')
Inputs may be any that keep to these rules, and one draw needn't show every extreme that they name: `page_table`: rows of a request's table up to page_count are distinct pages; slots beyond it hold 0 and are not part of the context. `page_count`: some request has 32 live slots and some has one.
All inputs are finite; a program needn't handle non-finite values.
Results may differ from a plain program's by a relative error of at most 0.013.
Values may be sent and summed in bfloat16 or wider, within the bound.
No kernel may reach another device: no remote copies, remote signals or barrier semaphores. Data moves between devices by JAX's collectives and lax.ppermute only.
A program may use at most 64 MiB of HBM per device.

v0:
```python
import math
import jax
import jax.numpy as jnp
from jax import lax
from jax.sharding import Mesh
from jax.sharding import PartitionSpec as P

H = 64
KVH = 8
HD = 128
LANES = 128


def split_pair(value):
    high = lax.reduce_precision(value, exponent_bits=8, mantissa_bits=7)
    low = lax.reduce_precision(value - high, exponent_bits=8, mantissa_bits=7)
    return (high, low)


def body(queries, key_pool, value_pool, page_table, page_count):
    n_page = lax.axis_size("page")
    n_yh = lax.axis_size("yh")
    n_xc = lax.axis_size("xc")
    page_index = lax.axis_index("page")
    yh_index = lax.axis_index("yh")
    pages_held = key_pool.shape[0]
    page_len = key_pool.shape[1]
    per_kv = H // KVH
    own_heads = H // n_page
    rows = queries.shape[0]
    score_scale = 1.0 / math.sqrt(HD)
    row_pages = n_yh * n_xc * pages_held
    row_ids = page_index * row_pages + jnp.arange(row_pages, dtype=jnp.int32)
    slot_live = jnp.arange(page_table.shape[1], dtype=jnp.int32)[None, :] < page_count[:, None]
    row_hit = jnp.any(
        (page_table[:, :, None] == row_ids[None, None, :]) & slot_live[:, :, None], axis=1
    )
    mask_cols = -(-row_pages // LANES) * LANES
    row_hit = jnp.pad(row_hit.astype(queries.dtype), ((0, 0), (0, mask_cols - row_pages)))
    packed = jnp.concatenate([queries, row_hit], axis=1)
    all_packed = lax.all_gather(packed, "yh", tiled=True)
    keys = lax.all_gather(key_pool, "xc", tiled=True)
    values = lax.all_to_all(
        jnp.broadcast_to(value_pool[None], (n_xc,) + value_pool.shape).reshape(
            (n_xc * pages_held,) + value_pool.shape[1:]
        ),
        "xc",
        0,
        0,
        tiled=True,
    )
    req_rows = all_packed.shape[0]
    all_q = all_packed[:, : H * HD]
    held = n_xc * pages_held
    page_hit = lax.dynamic_slice_in_dim(all_packed, H * HD + yh_index * held, held, 1) > 0.5
    token_hit = jnp.repeat(page_hit, page_len, axis=1)[:, None, None, :]
    grouped = all_q.reshape(req_rows, KVH, per_kv, HD)
    token_keys = keys.reshape(-1, KVH, HD)
    token_values = values.reshape(-1, KVH, HD)
    scores = (
        jnp.einsum("rkgd,tkd->rkgt", grouped, token_keys, preferred_element_type=jnp.float32)
        * score_scale
    )
    scores = jnp.where(token_hit, scores, jnp.float32(-1e30))
    max_hi, max_lo = split_pair(jnp.max(scores, axis=3))
    local_max = max_hi + max_lo
    exp_terms = jnp.where(token_hit, jnp.exp(scores - local_max[..., None]), jnp.float32(0.0))
    local_sum = jnp.sum(exp_terms, axis=3)
    weights = exp_terms.astype(jnp.bfloat16)
    local_out = jnp.einsum(
        "rkgt,tkd->rkgd", weights, token_values, preferred_element_type=jnp.float32
    )
    n_blocks = n_page * n_yh
    block_rows = rows * own_heads
    out_blocks = local_out.astype(jnp.bfloat16)
    out_blocks = out_blocks.reshape(n_yh, rows, n_page, own_heads, HD).transpose(2, 0, 1, 3, 4)
    out_blocks = out_blocks.reshape(n_blocks, block_rows, HD)
    sum_hi, sum_lo = split_pair(local_sum)

    def to_blocks(stat):
        stat = (
            stat.astype(jnp.bfloat16).reshape(n_yh, rows, n_page, own_heads).transpose(2, 0, 1, 3)
        )
        return stat.reshape(n_blocks, block_rows)

    stat_cols = -(-4 * block_rows // HD) * HD
    stats = jnp.concatenate(
        [to_blocks(max_hi), to_blocks(max_lo), to_blocks(sum_hi), to_blocks(sum_lo)]
        + [jnp.zeros((n_blocks, stat_cols - 4 * block_rows), jnp.bfloat16)],
        axis=1,
    )
    payload = jnp.concatenate([out_blocks, stats.reshape(n_blocks, -1, HD)], axis=1)
    arrived = lax.all_to_all(payload, ("page", "yh"), 0, 0, tiled=True)
    part_out = arrived[:, :block_rows, :].astype(jnp.float32)
    part_stats = arrived[:, block_rows:, :].reshape(n_blocks, stat_cols).astype(jnp.float32)
    part_max = part_stats[:, :block_rows] + part_stats[:, block_rows : 2 * block_rows]
    part_sum = (
        part_stats[:, 2 * block_rows : 3 * block_rows]
        + part_stats[:, 3 * block_rows : 4 * block_rows]
    )
    joint_max = jnp.max(part_max, axis=0)
    factor = jnp.exp(part_max - joint_max[None, :])
    joint_sum = jnp.sum(part_sum * factor, axis=0)
    joint_out = jnp.sum(part_out * factor[..., None], axis=0)
    result = joint_out / joint_sum[:, None]
    return result.reshape(rows, own_heads * HD).astype(jnp.bfloat16)


def solution(mesh):
    n_page, n_req = mesh.devices.shape
    n_yh = 2 if n_req % 2 == 0 else 1
    split = Mesh(mesh.devices.reshape(n_page, n_yh, n_req // n_yh), ("page", "yh", "xc"))
    req = ("yh", "xc")
    return jax.shard_map(
        body,
        mesh=split,
        in_specs=(
            P(req, None),
            P(("page",) + req, None, None),
            P(("page",) + req, None, None),
            P(req, None),
            P(req),
        ),
        out_specs=P(req, "page"),
        check_vma=False,
    )
```

profile of v0, /device:TPU:64, one launch (start us, length us, event | category | flops | bytes accessed | tf_op | source)
XLA Modules:
  0.0 122.1 jit_solution(18207185544669441702)
XLA Ops:
  6.5 0.7 all-gather.2.cloned.1.call-update
  7.3 2.5 %reshape.90 = bf16[8,128,1024]{2,1,0:T(8,128)(2,1)} broadcast(bf16[128,1024]{1,0:T(8,128)(2,1)} %bitcast.89), dimensions={1,2} | broadcast | bytes 2359296 | tf_op jit(solution)/shard_map/reshape | solution.py:44
  9.8 4.3 %all-to-all-start = ((bf16[8,128,1024]{2,1,0:T(8,128)(2,1)}), bf16[8,128,1024]{2,1,0:T(8,128)(2,1)S(1)}, u32[]{:S(2)}, u32[]{:S(2)}) async-start(bf16[8,128,1024]{2,1,0:T(8,128)(2,1)} %reshape.90), calls=%async_computation | async-start | bytes 4194304 | tf_op jit(solution)/shard_map/all_to_all | solution.py:43
  14.1 0.7 iota_compare_fusion
  14.8 1.1 and_reduce_fusion
  15.9 1.0 pad_maximum_fusion.1
  16.9 15.4 %all_gather.6 = bf16[32,8320]{1,0:T(8,128)(2,1)S(1)} all-gather(bf16[16,8320]{1,0:T(8,128)(2,1)S(1)} %pad_maximum_fusion.1), channel_id=1, replica_groups=mesh['page'=32,'yh'=2,'xc'=8] {'yh'}, dimensions={0}, use_global_device_ids=true | all-gather | bytes 798720 | tf_op jit(solution)/shard_map/all_gather | solution.py:41
  32.7 17.0 %all-to-all-done = bf16[8,128,1024]{2,1,0:T(8,128)(2,1)S(1)} async-done(((bf16[8,128,1024]{2,1,0:T(8,128)(2,1)}), bf16[8,128,1024]{2,1,0:T(8,128)(2,1)S(1)}, u32[]{:S(2)}, u32[]{:S(2)}) %all-to-all-start) | async-done | bytes 2097184 | tf_op jit(solution)/shard_map/all_to_all | solution.py:43
  49.7 2.0 %copy.71 = bf16[128,8,8,128]{3,2,1,0:T(8,128)(2,1)} copy(bf16[128,8,8,128]{3,1,2,0:T(8,128)(2,1)S(1)} %bitcast.78) | data formatting | bytes 4194304
  51.7 2.2 %copy.70 = bf16[128,8,8,128]{3,2,1,0:T(8,128)(2,1)S(1)} copy(bf16[128,8,8,128]{3,1,2,0:T(8,128)(2,1)} %bitcast.81) | data formatting | bytes 4194304
  53.9 5.1 %bitcast_reduce_fusion = (f32[32,8,8]{2,0,1:T(8,128)S(1)}, f32[8,32,8,1024]{3,2,1,0:T(8,128)}) fusion(pred[32,1024]{1,0:T(8,128)(4,1)S(1)} %bitcast.86, bf16[1024,8,128,1]{2,1,0,3:T(8,128)(2,1)S(1)} %bitcast.77, bf16[32,8,8,128]{3,2,1,0:T(8,128)(2,1)S(1)} %bitcast.79), kind=kOutput, calls=%fused_computation.1 | convolution fusion | flops 543160320 | bytes 11051008 | tf_op jit(solution)/shard_map/rkgd,tkd->rkgt/dot_general | solution.py:61
  59.3 5.3 %fusion.2 = f32[32,8,8]{2,0,1:T(8,128)S(1)} fusion(f32[8,32,8,1024]{3,2,1,0:T(8,128)} %get-tuple-element.12, f32[32,8,8]{2,0,1:T(8,128)S(1)} %copy.48, pred[32,1024]{1,0:T(8,128)(4,1)S(1)} %bitcast.87), kind=kLoop, calls=%fused_computation.5 | loop fusion | flops 10483712 | bytes 8437760 | tf_op jit(solution)/shard_map/reduce_sum | solution.py:68
  64.9 0.6 copy.56
  65.5 0.3 reshape.96
  65.9 0.6 copy.57
  66.5 0.3 reshape.97
  66.9 0.6 copy.53
  67.5 0.3 reshape.94
  67.8 0.6 copy.54
  68.9 5.9 %fusion.16 = bf16[32,8,8,128]{3,2,0,1:T(8,128)(2,1)S(1)} fusion(bf16[1024,8,128,1]{2,1,0,3:T(8,128)(2,1)S(1)} %bitcast.82, f32[8,32,8,1024]{3,2,1,0:T(8,128)} %get-tuple-element.12, f32[32,8,8]{2,0,1:T(8,128)S(1)} %copy.48, pred[32,1024]{1,0:T(8,128)(4,1)S(1)} %bitcast.88), kind=kOutput, calls=%fused_computation.14 | convolution fusion | flops 547618816 | bytes 11051008 | tf_op jit(solution)/shard_map/rkgt,tkd->rkgd/dot_general | solution.py:70
  74.9 0.5 copy.51
  75.5 38.4 %all_to_all.10 = bf16[64,33,128]{2,1,0:T(8,128)(2,1)S(1)} all-to-all(bf16[64,33,128]{2,1,0:T(8,128)(2,1)S(1)} %pad_maximum_fusion), channel_id=1, replica_groups=mesh['page'=32,'yh'=2,'xc'=8] {'page','yh'}, dimensions={0} | all-to-all | bytes 1081344 | tf_op jit(solution)/shard_map/all_to_all | solution.py:93
  114.2 0.3 multiply_reduce_fusion
  114.7 0.6 fusion.33
  (30 shorter events, 1.9 us)
Async XLA Ops:
  6.5 45.1 %all-gather.2.cloned.1.call-start = ((), (), s32[]{:S(2)}) async-start(), calls=%async_computation.2 | async-start | bytes 2359296 | tf_op jit(solution)/shard_map/all_gather | solution.py:42
  9.8 39.9 %all-to-all-start = ((bf16[8,128,1024]{2,1,0:T(8,128)(2,1)}), bf16[8,128,1024]{2,1,0:T(8,128)(2,1)S(1)}, u32[]{:S(2)}, u32[]{:S(2)}) async-start(bf16[8,128,1024]{2,1,0:T(8,128)(2,1)} %reshape.90), calls=%async_computation | async-start | bytes 4194304 | tf_op jit(solution)/shard_map/all_to_all | solution.py:43
  59.0 9.9 %copy-start = (bf16[128,8,8,128]{3,2,1,0:T(8,128)(2,1)S(1)}, bf16[128,8,8,128]{3,2,1,0:T(8,128)(2,1)}, u32[]{:S(2)}) copy-start(bf16[128,8,8,128]{3,2,1,0:T(8,128)(2,1)} %copy.71) | copy-start | bytes 6291460
Sparse Core Ops, SparseCore 0:
  9.5 40.7 all-gather.1
where the time goes:
time: 123 us; the launch traced here: 122 us
  blocking collectives  53.8 us (44%)
  waiting for transfers between devices  17.7 us (14%)
  between operations  13.6 us (11%)
  local copies, waits for them, and re-layouts  12.1 us (10%)
  matrix products  11 us (9%)
  other arithmetic  9.6 us (8%)
  starting transfers between devices  4.3 us (3%)
    all_to_all x1, blocking collectives, body(): arrived = lax.all_to_all(payload, ('page', 'yh'), 0, 0, tiled=True)  38.4 us
    all_to_all x1, waiting for transfers between devices, body(): lax.all_to_all(jnp.broadcast_to(value_pool[None], (n_xc,) + value_pool.sh...  17 us
    all_gather x1, blocking collectives, body(): all_packed = lax.all_gather(packed, 'yh', tiled=True)  15.4 us
    dot_general x1, matrix products, body(): jnp.einsum('rkgt,tkd->rkgd', weights, token_values, preferred_element_typ...  5.88 us
    reduce_sum x1, other arithmetic, body(): local_sum = jnp.sum(exp_terms, axis=3)  5.32 us
    dot_general x1, matrix products, body(): jnp.einsum('rkgd,tkd->rkgt', grouped, token_keys, preferred_element_type=...  5.13 us
    unnamed x7, local copies, waits for them, and re-layouts  4.4 us
    all_to_all x1, starting transfers between devices, body(): lax.all_to_all(jnp.broadcast_to(value_pool[None], (n_xc,) + value_pool.sh...  4.3 us
  transfers between devices with their start and end apart: 2, of which 1 were waited for; matrix products, arithmetic and copies ran while one was open for 6% of the time, Pallas kernels for 0%

commit v1 on v0

--- a/solution.py
+++ b/solution.py
@@ -38,7 +38,9 @@
     mask_cols = -(-row_pages // LANES) * LANES
     row_hit = jnp.pad(row_hit.astype(queries.dtype), ((0, 0), (0, mask_cols - row_pages)))
     packed = jnp.concatenate([queries, row_hit], axis=1)
-    all_packed = lax.all_gather(packed, "yh", tiled=True)
+    all_packed = jnp.concatenate(
+        lax.all_to_all(jnp.stack([packed] * lax.axis_size("yh"), 0), "yh", 0, 0), 0
+    )
     keys = lax.all_gather(key_pool, "xc", tiled=True)
     values = lax.all_to_all(
         jnp.broadcast_to(value_pool[None], (n_xc,) + value_pool.shape).reshape(

time: 123 us -> 136 us (1.11)
  waiting for transfers between devices: 17.7 us -> 27.5 us
  blocking collectives: 53.8 us -> 57.8 us
    all_to_all x0 -> x1, blocking collectives: none -> 23 us  [body(): lax.all_to_all(jnp.stack([packed] * lax.axis_size('yh'), 0), 'yh', 0, 0)]
    all_gather x1 -> x0, blocking collectives: 15.4 us -> none  [body(): all_packed = lax.all_gather(packed, 'yh', tiled=True)]
    all_to_all x1, waiting for transfers between devices: 17 us -> 26.8 us  [body(): lax.all_to_all(jnp.broadcast_to(value_pool[None], (n_xc,) + value_pool.sh...]
    all_to_all x1, blocking collectives: 38.4 us -> 34.8 us  [body(): arrived = lax.all_to_all(payload, ('page', 'yh'), 0, 0, tiled=True)]
where the time goes in v1:
time: 136 us
  blocking collectives  57.8 us (42%)
  waiting for transfers between devices  27.5 us (20%)
  between operations  13.6 us (10%)
  local copies, waits for them, and re-layouts  12.1 us (9%)
  matrix products  11 us (8%)
  other arithmetic  9.65 us (7%)
  starting transfers between devices  4.3 us (3%)
    all_to_all x1, blocking collectives, body(): arrived = lax.all_to_all(payload, ('page', 'yh'), 0, 0, tiled=True)  34.8 us
    all_to_all x1, waiting for transfers between devices, body(): lax.all_to_all(jnp.broadcast_to(value_pool[None], (n_xc,) + value_pool.sh...  26.8 us
    all_to_all x1, blocking collectives, body(): lax.all_to_all(jnp.stack([packed] * lax.axis_size('yh'), 0), 'yh', 0, 0)  23 us
    dot_general x1, matrix products, body(): jnp.einsum('rkgt,tkd->rkgd', weights, token_values, preferred_element_typ...  5.9 us
    reduce_sum x1, other arithmetic, body(): local_sum = jnp.sum(exp_terms, axis=3)  5.33 us
    dot_general x1, matrix products, body(): jnp.einsum('rkgd,tkd->rkgt', grouped, token_keys, preferred_element_type=...  5.13 us
    unnamed x7, local copies, waits for them, and re-layouts  4.4 us
    all_to_all x1, starting transfers between devices, body(): lax.all_to_all(jnp.broadcast_to(value_pool[None], (n_xc,) + value_pool.sh...  4.3 us
  transfers between devices with their start and end apart: 2, of which 1 were waited for; matrix products, arithmetic and copies ran while one was open for 6% of the time, Pallas kernels for 0%

profile of v1, /device:TPU:64, one launch (start us, length us, event | category | flops | bytes accessed | tf_op | source)
XLA Modules:
  0.0 136.1 jit_solution(3449780425088390809)
XLA Ops:
  6.5 0.7 all-gather.2.cloned.1.call-update
  7.3 0.7 iota_compare_fusion
  8.0 1.1 and_reduce_fusion
  9.1 1.0 maximum_bitcast_fusion
  10.2 23.0 %all_to_all.15 = bf16[2,16,8320]{2,1,0:T(8,128)(2,1)S(1)} all-to-all(bf16[2,16,8320]{2,1,0:T(8,128)(2,1)S(1)} %pad_maximum_fusion.1), channel_id=1, replica_groups=mesh['page'=32,'yh'=2,'xc'=8] {'yh'}, dimensions={0} | all-to-all | bytes 1064960 | tf_op jit(solution)/shard_map/all_to_all | solution.py:42
  33.2 2.5 %reshape.94 = bf16[8,128,1024]{2,1,0:T(8,128)(2,1)} broadcast(bf16[128,1024]{1,0:T(8,128)(2,1)} %bitcast.94), dimensions={1,2} | broadcast | bytes 2359296 | tf_op jit(solution)/shard_map/reshape | solution.py:46
  35.7 4.3 %all-to-all-start.1 = ((bf16[8,128,1024]{2,1,0:T(8,128)(2,1)}), bf16[8,128,1024]{2,1,0:T(8,128)(2,1)S(1)}, u32[]{:S(2)}, u32[]{:S(2)}) async-start(bf16[8,128,1024]{2,1,0:T(8,128)(2,1)} %reshape.94), calls=%async_computation.1 | async-start | bytes 4194304 | tf_op jit(solution)/shard_map/all_to_all | solution.py:45
  40.3 26.8 %all-to-all-done.1 = bf16[8,128,1024]{2,1,0:T(8,128)(2,1)S(1)} async-done(((bf16[8,128,1024]{2,1,0:T(8,128)(2,1)}), bf16[8,128,1024]{2,1,0:T(8,128)(2,1)S(1)}, u32[]{:S(2)}, u32[]{:S(2)}) %all-to-all-start.1) | async-done | bytes 2097184 | tf_op jit(solution)/shard_map/all_to_all | solution.py:45
  67.1 2.0 %copy.71 = bf16[128,8,8,128]{3,2,1,0:T(8,128)(2,1)} copy(bf16[128,8,8,128]{3,1,2,0:T(8,128)(2,1)S(1)} %bitcast.81) | data formatting | bytes 4194304
  69.1 2.2 %copy.70 = bf16[128,8,8,128]{3,2,1,0:T(8,128)(2,1)S(1)} copy(bf16[128,8,8,128]{3,1,2,0:T(8,128)(2,1)} %bitcast.86) | data formatting | bytes 4194304
  71.4 5.1 %bitcast_reduce_fusion = (f32[32,8,8]{2,0,1:T(8,128)S(1)}, f32[8,32,8,1024]{3,2,1,0:T(8,128)}) fusion(pred[32,1024]{1,0:T(8,128)(4,1)S(1)} %bitcast.91, bf16[1024,8,128,1]{2,1,0,3:T(8,128)(2,1)S(1)} %bitcast.80, bf16[32,8,8,128]{3,2,1,0:T(8,128)(2,1)S(1)} %bitcast.82), kind=kOutput, calls=%fused_computation.1 | convolution fusion | flops 543160320 | bytes 11051008 | tf_op jit(solution)/shard_map/rkgd,tkd->rkgt/dot_general | solution.py:63
  76.8 5.3 %fusion.2 = f32[32,8,8]{2,0,1:T(8,128)S(1)} fusion(f32[8,32,8,1024]{3,2,1,0:T(8,128)} %get-tuple-element.12, f32[32,8,8]{2,0,1:T(8,128)S(1)} %copy.48, pred[32,1024]{1,0:T(8,128)(4,1)S(1)} %bitcast.92), kind=kLoop, calls=%fused_computation.5 | loop fusion | flops 10483712 | bytes 8437760 | tf_op jit(solution)/shard_map/reduce_sum | solution.py:70
  82.4 0.6 copy.56
  83.0 0.3 reshape.100
  83.4 0.6 copy.57
  84.0 0.3 reshape.101
  84.4 0.6 copy.53
  85.0 0.3 reshape.98
  85.3 0.6 copy.54
  86.4 5.9 %fusion.16 = bf16[32,8,8,128]{3,2,0,1:T(8,128)(2,1)S(1)} fusion(bf16[1024,8,128,1]{2,1,0,3:T(8,128)(2,1)S(1)} %bitcast.87, f32[8,32,8,1024]{3,2,1,0:T(8,128)} %get-tuple-element.12, f32[32,8,8]{2,0,1:T(8,128)S(1)} %copy.48, pred[32,1024]{1,0:T(8,128)(4,1)S(1)} %bitcast.93), kind=kOutput, calls=%fused_computation.14 | convolution fusion | flops 547618816 | bytes 11051008 | tf_op jit(solution)/shard_map/rkgt,tkd->rkgd/dot_general | solution.py:72
  92.4 0.5 copy.51
  93.0 34.8 %all_to_all.16 = bf16[64,33,128]{2,1,0:T(8,128)(2,1)S(1)} all-to-all(bf16[64,33,128]{2,1,0:T(8,128)(2,1)S(1)} %pad_maximum_fusion), channel_id=1, replica_groups=mesh['page'=32,'yh'=2,'xc'=8] {'page','yh'}, dimensions={0} | all-to-all | bytes 1081344 | tf_op jit(solution)/shard_map/all_to_all | solution.py:95
  128.1 0.3 multiply_reduce_fusion
  128.6 0.6 fusion.33
  (31 shorter events, 2.0 us)
Async XLA Ops:
  6.5 62.6 %all-gather.2.cloned.1.call-start = ((), (), s32[]{:S(2)}) async-start(), calls=%async_computation.3 | async-start | bytes 2359296 | tf_op jit(solution)/shard_map/all_gather | solution.py:44
  35.7 31.5 %all-to-all-start.1 = ((bf16[8,128,1024]{2,1,0:T(8,128)(2,1)}), bf16[8,128,1024]{2,1,0:T(8,128)(2,1)S(1)}, u32[]{:S(2)}, u32[]{:S(2)}) async-start(bf16[8,128,1024]{2,1,0:T(8,128)(2,1)} %reshape.94), calls=%async_computation.1 | async-start | bytes 4194304 | tf_op jit(solution)/shard_map/all_to_all | solution.py:45
  76.5 9.9 %copy-start = (bf16[128,8,8,128]{3,2,1,0:T(8,128)(2,1)S(1)}, bf16[128,8,8,128]{3,2,1,0:T(8,128)(2,1)}, u32[]{:S(2)}) copy-start(bf16[128,8,8,128]{3,2,1,0:T(8,128)(2,1)} %copy.71) | copy-start | bytes 6291460
Sparse Core Ops, SparseCore 0:
  9.5 34.5 all-gather.1
